TPU v7x, 32 devices: a whole 2x2x4 slice. The times are simulated.
32 devices in a mesh: rows: 4 (over y, x), cols: 8 (over z, core).
Axes of the slice: x: 2, y: 2, z: 4, core: 2. Of those that a mesh axis runs over, the one named last changes fastest.
Arguments:
- frames: bfloat16 [2, 16, 8192], P(None, 'rows', 'cols'), may hold values from -6 to 6
- hidden_start: bfloat16 [16, 256, 128], P('rows', 'cols'), may hold values from -3 to 3
- cell_start: float32 [16, 256, 128], P('rows', 'cols'), may hold values from -6 to 6
- kernel: bfloat16 [1440, 512], replicated, may hold values from -0.15625 to 0.15625
- gate_bias: float32 [512], replicated, may hold values from -4 to 4
- cotangent: bfloat16 [2, 16, 256, 128], P(None, 'rows', 'cols'), may hold values from -6 to 6
Outputs:
- hidden_final: bfloat16 [16, 256, 128], P('rows', 'cols')
- grad_hidden_start: float32 [16, 256, 128], P('rows', 'cols')
- grad_cell_start: float32 [16, 256, 128], P('rows', 'cols')
- kernel_grad: float32 [1440, 512], replicated
- bias_grad: float32 [512], replicated
All inputs are finite; a program needn't handle non-finite values.
Results may differ from a plain program's by a relative error of at most 0.015.
Values may be sent and summed in bfloat16 or wider, within the bound.
No kernel may reach another device: no remote copies, remote signals or barrier semaphores. Data moves between devices by JAX's collectives and lax.ppermute only.
A program may use at most 64 MiB of HBM per device.

v0:
```python
import math
import jax
import jax.numpy as jnp
from jax import lax
from jax.sharding import PartitionSpec as P

HC = 128
CI = 32
KS = 3
STEPS = 2
GATES = 512
KIN = 1440


def extended(cells, sides, width):
    for axis, dim in sides:
        count = lax.axis_size(axis)
        ends = count - 1
        head = lax.slice_in_dim(cells, 0, width, axis=dim)
        tail = lax.slice_in_dim(cells, cells.shape[dim] - width, cells.shape[dim], axis=dim)
        cells = jnp.concatenate(
            [
                lax.ppermute(tail, axis, [(i, (i + 1) % count) for i in range(ends)]),
                cells,
                lax.ppermute(head, axis, [((i + 1) % count, i) for i in range(ends)]),
            ],
            axis=dim,
        )
    return cells


def tap_columns(padded, rows_dev, cols_dev, reverse):
    pieces = []
    for tap_row in range(KS):
        for tap_col in range(KS):
            if reverse:
                first_row = KS - 1 - tap_row
                first_col = KS - 1 - tap_col
            else:
                first_row = tap_row
                first_col = tap_col
            pieces.append(
                padded[first_row : first_row + rows_dev, first_col : first_col + cols_dev]
            )
    joined = jnp.concatenate(pieces, axis=-1)
    return joined.reshape(rows_dev * cols_dev, joined.shape[-1])


def shards(frames, hidden_start, cell_start, kernel, gate_bias, cotangent):
    rows_dev = hidden_start.shape[0]
    cols_dev = hidden_start.shape[1]
    chans = CI + HC
    taps = KS * KS
    cells = rows_dev * cols_dev
    hidden = hidden_start
    cell = cell_start
    saved = []
    for moment in range(STEPS):
        inputs = frames[moment].reshape(rows_dev, cols_dev, CI)
        stacked = jnp.concatenate([inputs, hidden], axis=-1)
        padded = extended(stacked, (("rows", 0), ("cols", 1)), 1)
        patches = tap_columns(padded, rows_dev, cols_dev, False)
        gates = jnp.dot(patches, kernel, preferred_element_type=jnp.float32) + gate_bias
        gates = gates.reshape(rows_dev, cols_dev, GATES)
        gate_in = jax.nn.sigmoid(gates[..., :HC])
        gate_forget = jax.nn.sigmoid(gates[..., HC : 2 * HC])
        gate_cand = jnp.tanh(gates[..., 2 * HC : 3 * HC])
        gate_out = jax.nn.sigmoid(gates[..., 3 * HC :])
        cell_prev = cell
        cell = gate_forget * cell_prev + gate_in * gate_cand
        hidden = (gate_out * jnp.tanh(cell)).astype(jnp.bfloat16)
        saved.append((patches, gate_in, gate_forget, gate_cand, gate_out, cell_prev, cell))
    blocks = kernel.reshape(taps, chans, GATES)
    adjoint_matrix = jnp.transpose(blocks, (0, 2, 1)).reshape(taps * GATES, chans)
    grad_hidden = cotangent[STEPS - 1].astype(jnp.float32)
    grad_cell = jnp.zeros((rows_dev, cols_dev, HC), jnp.float32)
    kernel_acc = jnp.zeros((KIN, GATES), jnp.float32)
    bias_acc = jnp.zeros((GATES,), jnp.float32)
    for moment in range(STEPS - 1, -1, -1):
        patches, gate_in, gate_forget, gate_cand, gate_out, cell_prev, cell_now = saved[moment]
        tanh_cell = jnp.tanh(cell_now)
        summed = grad_cell + grad_hidden * gate_out * (1.0 - tanh_cell * tanh_cell)
        pre_in = summed * gate_cand * gate_in * (1.0 - gate_in)
        pre_forget = summed * cell_prev * gate_forget * (1.0 - gate_forget)
        pre_cand = summed * gate_in * (1.0 - gate_cand * gate_cand)
        pre_out = grad_hidden * tanh_cell * gate_out * (1.0 - gate_out)
        grad_cell = summed * gate_forget
        grad_gates = jnp.concatenate([pre_in, pre_forget, pre_cand, pre_out], axis=-1).astype(
            jnp.bfloat16
        )
        flat_grads = grad_gates.reshape(cells, GATES)
        kernel_acc = kernel_acc + jnp.dot(patches.T, flat_grads, preferred_element_type=jnp.float32)
        bias_acc = bias_acc + jnp.sum(flat_grads.astype(jnp.float32), axis=0)
        grad_padded = extended(grad_gates, (("rows", 0), ("cols", 1)), 1)
        reversed_cols = tap_columns(grad_padded, rows_dev, cols_dev, True)
        grad_stacked = jnp.dot(reversed_cols, adjoint_matrix, preferred_element_type=jnp.float32)
        grad_stacked = grad_stacked.reshape(rows_dev, cols_dev, chans)
        grad_hidden = grad_stacked[..., CI:]
        if moment > 0:
            grad_hidden = grad_hidden + cotangent[moment - 1].astype(jnp.float32)
    kernel_total, bias_total = lax.psum((kernel_acc, bias_acc), ("rows", "cols"))
    total_cells = STEPS * rows_dev * lax.axis_size("rows") * cols_dev * lax.axis_size("cols")
    norm_scale = 1.0 / math.sqrt(total_cells)
    return (hidden, grad_hidden, grad_cell, kernel_total * norm_scale, bias_total * norm_scale)


def solution(mesh):
    placed = (
        P(None, "rows", "cols"),
        P("rows", "cols", None),
        P("rows", "cols", None),
        P(),
        P(),
        P(None, "rows", "cols", None),
    )
    return jax.shard_map(
        shards,
        mesh=mesh,
        in_specs=placed,
        out_specs=(
            P("rows", "cols", None),
            P("rows", "cols", None),
            P("rows", "cols", None),
            P(),
            P(),
        ),
        check_vma=False,
    )
```

profile of v0, /device:TPU:0, one launch (start us, length us, event | category | flops | bytes accessed | tf_op | source)
XLA Modules:
  0.0 274.6 jit_solution(14365913064977950264)
XLA Ops:
  8.8 4.8 %collective-permute-start = (bf16[1,32,160]{2,1,0:T(8,128)(2,1)S(1)}, bf16[1,32,160]{2,1,0:T(8,128)(2,1)S(1)}, u32[]{:S(2)}, u32[]{:S(2)}) collective-permute-start(bf16[1,32,160]{2,1,0:T(8,128)(2,1)S(1)} %get-tuple-element.60), channel_id=1, source_target_pairs={{0,8},{8,16},{16,24},{1,9},{9,17},{17,25},{2,10},{10,18},{18,26},{... | collective-permute-start | bytes 30728 | tf_op jit(solution)/shard_map/ppermute | solution.py:23
  13.7 1.3 collective-permute-start.1
  15.2 4.1 %collective-permute-done.1 = bf16[1,32,160]{2,1,0:T(8,128)(2,1)S(1)} collective-permute-done((bf16[1,32,160]{2,1,0:T(8,128)(2,1)S(1)}, bf16[1,32,160]{2,1,0:T(8,128)(2,1)S(1)}, u32[]{:S(2)}, u32[]{:S(2)}) %collective-permute-start.1) | collective-permute-done | bytes 10272 | tf_op jit(solution)/shard_map/ppermute | solution.py:25
  20.1 1.3 collective-permute-start.3
  21.4 3.2 %collective-permute-start.2 = (bf16[6,1,160]{2,1,0:T(2,128)(2,1)S(1)}, bf16[6,1,160]{2,1,0:T(2,128)(2,1)S(1)}, u32[]{:S(2)}, u32[]{:S(2)}) collective-permute-start(bf16[6,1,160]{2,1,0:T(2,128)(2,1)S(1)} %get-tuple-element.53), channel_id=1, source_target_pairs={{0,1},{1,2},{2,3},{3,4},{4,5},{5,6},{6,7},{8,9},{9,10},{10,11},{11... | collective-permute-start | bytes 5768 | tf_op jit(solution)/shard_map/ppermute | solution.py:23
  24.6 0.9 pad_maximum_fusion.24
  25.6 0.9 pad_maximum_fusion.18
  27.9 4.3 %collective-permute-start.4 = (bf16[1,32,160]{2,1,0:T(8,128)(2,1)S(1)}, bf16[1,32,160]{2,1,0:T(8,128)(2,1)S(1)}, u32[]{:S(2)}, u32[]{:S(2)}) collective-permute-start(bf16[1,32,160]{2,1,0:T(8,128)(2,1)S(1)} %get-tuple-element.56), channel_id=1, source_target_pairs={{0,8},{8,16},{16,24},{1,9},{9,17},{17,25},{2,10},{10,18},{18,26},{... | collective-permute-start | bytes 30728 | tf_op jit(solution)/shard_map/ppermute | solution.py:23
  32.2 1.3 collective-permute-start.5
  33.6 4.3 %collective-permute-done.5 = bf16[1,32,160]{2,1,0:T(8,128)(2,1)S(1)} collective-permute-done((bf16[1,32,160]{2,1,0:T(8,128)(2,1)S(1)}, bf16[1,32,160]{2,1,0:T(8,128)(2,1)S(1)}, u32[]{:S(2)}, u32[]{:S(2)}) %collective-permute-start.5) | collective-permute-done | bytes 10272 | tf_op jit(solution)/shard_map/ppermute | solution.py:25
  38.0 1.3 collective-permute-start.7
  39.3 3.0 %collective-permute-start.6 = (bf16[6,1,160]{2,1,0:T(2,128)(2,1)S(1)}, bf16[6,1,160]{2,1,0:T(2,128)(2,1)S(1)}, u32[]{:S(2)}, u32[]{:S(2)}) collective-permute-start(bf16[6,1,160]{2,1,0:T(2,128)(2,1)S(1)} %get-tuple-element.49), channel_id=1, source_target_pairs={{0,1},{1,2},{2,3},{3,4},{4,5},{5,6},{6,7},{8,9},{9,10},{10,11},{11... | collective-permute-start | bytes 5768 | tf_op jit(solution)/shard_map/ppermute | solution.py:23
  45.9 3.4 %collective-permute-start.8 = (bf16[1,32,512]{2,1,0:T(8,128)(2,1)S(1)}, bf16[1,32,512]{2,1,0:T(8,128)(2,1)S(1)}, u32[]{:S(2)}, u32[]{:S(2)}) collective-permute-start(bf16[1,32,512]{2,1,0:T(8,128)(2,1)S(1)} %get-tuple-element.32), channel_id=1, source_target_pairs={{0,8},{8,16},{16,24},{1,9},{9,17},{17,25},{2,10},{10,18},{18,26},{... | collective-permute-start | bytes 98312 | tf_op jit(solution)/shard_map/ppermute | solution.py:23
  49.3 1.3 collective-permute-start.9
  50.6 2.5 copy.14
  53.1 4.0 %reshape.83 = bf16[4608,160,1]{0,1,2:T(8,128)(2,1)} reshape(bf16[9,512,160]{1,0,2:T(8,128)(2,1)} %bitcast.57) | data formatting | bytes 2949120 | tf_op jit(solution)/shard_map/reshape | solution.py:74
  57.4 4.2 %collective-permute-start.11 = (bf16[6,1,512]{2,1,0:T(2,128)(2,1)S(1)}, bf16[6,1,512]{2,1,0:T(2,128)(2,1)S(1)}, u32[]{:S(2)}, u32[]{:S(2)}) collective-permute-start(bf16[6,1,512]{2,1,0:T(2,128)(2,1)S(1)} %get-tuple-element.28), channel_id=1, source_target_pairs={{0,1},{1,2},{2,3},{3,4},{4,5},{5,6},{6,7},{8,9},{9,10},{10,11},{11... | collective-permute-start | bytes 18440 | tf_op jit(solution)/shard_map/ppermute | solution.py:23
  61.6 1.3 collective-permute-start.10
  63.3 3.5 %collective-permute-done.10 = bf16[6,1,512]{2,1,0:T(2,128)(2,1)S(1)} collective-permute-done((bf16[6,1,512]{2,1,0:T(2,128)(2,1)S(1)}, bf16[6,1,512]{2,1,0:T(2,128)(2,1)S(1)}, u32[]{:S(2)}, u32[]{:S(2)}) %collective-permute-start.10) | collective-permute-done | bytes 6176 | tf_op jit(solution)/shard_map/ppermute | solution.py:25
  67.2 1.0 copy-done.1
  68.3 1.1 fusion.46
  69.5 4.5 %collective-permute-start.12 = (bf16[1,32,512]{2,1,0:T(8,128)(2,1)S(1)}, bf16[1,32,512]{2,1,0:T(8,128)(2,1)S(1)}, u32[]{:S(2)}, u32[]{:S(2)}) collective-permute-start(bf16[1,32,512]{2,1,0:T(8,128)(2,1)S(1)} %get-tuple-element.30), channel_id=1, source_target_pairs={{0,8},{8,16},{16,24},{1,9},{9,17},{17,25},{2,10},{10,18},{18,26},{... | collective-permute-start | bytes 98312 | tf_op jit(solution)/shard_map/ppermute | solution.py:23
  74.0 1.3 collective-permute-start.13
  75.9 2.2 fusion
  78.1 42.4 %psum.15 = f32[512]{0:T(512)S(1)} all-reduce(f32[512]{0:T(512)S(1)} %add.68), channel_id=1, replica_groups=mesh['rows'=4,'cols'=8] {'rows','cols'}, use_global_device_ids=true, to_apply=%region_3.0 | all-reduce | flops 512 | bytes 4096 | tf_op jit(solution)/shard_map/psum | solution.py:101
  120.5 1.3 collective-permute-start.15
  121.8 1.3 collective-permute-start.14
  123.7 2.0 collective-permute-done.14
  126.2 1.1 copy-done.2
  127.2 1.1 fusion.1
  128.3 135.6 %all-reduce.2.cloned.1.call-done = f32[1440,512]{1,0:T(8,128)} async-done(((f32[1440,512]{1,0:T(8,128)}), f32[1440,512]{1,0:T(8,128)}) %all-reduce.2.cloned.1.call-update) | async-done | bytes 2949136 | tf_op jit(solution)/shard_map/psum | solution.py:101
  263.9 3.8 %broadcast_multiply_fusion = f32[1440,512]{1,0:T(8,128)} fusion(f32[1440,512]{1,0:T(8,128)} %all-reduce.2.cloned.1.call-done), kind=kLoop, calls=%fused_computation.4 | loop fusion | flops 737280 | bytes 5898240 | tf_op jit(solution)/shard_map/mul | solution.py:104
  (105 shorter events, 10.2 us)
Async XLA Ops:
  7.2 19.4 %copy-start.3 = (bf16[4,32,128]{2,1,0:T(8,128)(2,1)S(1)}, bf16[4,32,128]{2,1,0:T(8,128)(2,1)}, u32[]{:S(2)}) copy-start(bf16[4,32,128]{2,1,0:T(8,128)(2,1)} %param.7) | copy-start | bytes 98308
  7.2 256.8 %all-reduce.2.cloned.1.call-start = ((), (), s32[]{:S(2)}) async-start(), calls=%async_computation | async-start | bytes 5898240 | tf_op jit(solution)/shard_map/psum | solution.py:101
  8.8 6.3 %collective-permute-start = (bf16[1,32,160]{2,1,0:T(8,128)(2,1)S(1)}, bf16[1,32,160]{2,1,0:T(8,128)(2,1)S(1)}, u32[]{:S(2)}, u32[]{:S(2)}) collective-permute-start(bf16[1,32,160]{2,1,0:T(8,128)(2,1)S(1)} %get-tuple-element.60), channel_id=1, source_target_pairs={{0,8},{8,16},{16,24},{1,9},{9,17},{17,25},{2,10},{10,18},{18,26},{... | collective-permute-start | bytes 30728 | tf_op jit(solution)/shard_map/ppermute | solution.py:23
  13.7 5.6 %collective-permute-start.1 = (bf16[1,32,160]{2,1,0:T(8,128)(2,1)S(1)}, bf16[1,32,160]{2,1,0:T(8,128)(2,1)S(1)}, u32[]{:S(2)}, u32[]{:S(2)}) collective-permute-start(bf16[1,32,160]{2,1,0:T(8,128)(2,1)S(1)} %get-tuple-element.61), channel_id=1, source_target_pairs={{8,0},{16,8},{24,16},{9,1},{17,9},{25,17},{10,2},{18,10},{26,18},{... | collective-permute-start | bytes 30728 | tf_op jit(solution)/shard_map/ppermute | solution.py:25
  20.1 5.4 %collective-permute-start.3 = (bf16[6,1,160]{2,1,0:T(2,128)(2,1)S(1)}, bf16[6,1,160]{2,1,0:T(2,128)(2,1)S(1)}, u32[]{:S(2)}, u32[]{:S(2)}) collective-permute-start(bf16[6,1,160]{2,1,0:T(2,128)(2,1)S(1)} %get-tuple-element.52), channel_id=1, source_target_pairs={{1,0},{2,1},{3,2},{4,3},{5,4},{6,5},{7,6},{9,8},{10,9},{11,10},{12... | collective-permute-start | bytes 5768 | tf_op jit(solution)/shard_map/ppermute | solution.py:25
  21.4 5.4 %copy-start = (bf16[1440,512]{1,0:T(8,128)(2,1)S(1)}, bf16[1440,512]{1,0:T(8,128)(2,1)}, u32[]{:S(2)}) copy-start(bf16[1440,512]{1,0:T(8,128)(2,1)} %param.9) | copy-start | bytes 4423684
  21.4 5.4 %copy-start.16 = (f32[512]{0:T(512)S(1)}, f32[512]{0:T(512)}, u32[]{:S(2)}) copy-start(f32[512]{0:T(512)} %param.10) | copy-start | bytes 6148
  21.4 4.1 %collective-permute-start.2 = (bf16[6,1,160]{2,1,0:T(2,128)(2,1)S(1)}, bf16[6,1,160]{2,1,0:T(2,128)(2,1)S(1)}, u32[]{:S(2)}, u32[]{:S(2)}) collective-permute-start(bf16[6,1,160]{2,1,0:T(2,128)(2,1)S(1)} %get-tuple-element.53), channel_id=1, source_target_pairs={{0,1},{1,2},{2,3},{3,4},{4,5},{5,6},{6,7},{8,9},{9,10},{10,11},{11... | collective-permute-start | bytes 5768 | tf_op jit(solution)/shard_map/ppermute | solution.py:23
  26.9 0.8 copy-start.12
  27.9 5.7 %collective-permute-start.4 = (bf16[1,32,160]{2,1,0:T(8,128)(2,1)S(1)}, bf16[1,32,160]{2,1,0:T(8,128)(2,1)S(1)}, u32[]{:S(2)}, u32[]{:S(2)}) collective-permute-start(bf16[1,32,160]{2,1,0:T(8,128)(2,1)S(1)} %get-tuple-element.56), channel_id=1, source_target_pairs={{0,8},{8,16},{16,24},{1,9},{9,17},{17,25},{2,10},{10,18},{18,26},{... | collective-permute-start | bytes 30728 | tf_op jit(solution)/shard_map/ppermute | solution.py:23
  32.2 5.8 %collective-permute-start.5 = (bf16[1,32,160]{2,1,0:T(8,128)(2,1)S(1)}, bf16[1,32,160]{2,1,0:T(8,128)(2,1)S(1)}, u32[]{:S(2)}, u32[]{:S(2)}) collective-permute-start(bf16[1,32,160]{2,1,0:T(8,128)(2,1)S(1)} %get-tuple-element.57), channel_id=1, source_target_pairs={{8,0},{16,8},{24,16},{9,1},{17,9},{25,17},{10,2},{18,10},{26,18},{... | collective-permute-start | bytes 30728 | tf_op jit(solution)/shard_map/ppermute | solution.py:25
  38.0 4.4 %collective-permute-start.7 = (bf16[6,1,160]{2,1,0:T(2,128)(2,1)S(1)}, bf16[6,1,160]{2,1,0:T(2,128)(2,1)S(1)}, u32[]{:S(2)}, u32[]{:S(2)}) collective-permute-start(bf16[6,1,160]{2,1,0:T(2,128)(2,1)S(1)} %get-tuple-element.48), channel_id=1, source_target_pairs={{1,0},{2,1},{3,2},{4,3},{5,4},{6,5},{7,6},{9,8},{10,9},{11,10},{12... | collective-permute-start | bytes 5768 | tf_op jit(solution)/shard_map/ppermute | solution.py:25
  39.3 3.8 %collective-permute-start.6 = (bf16[6,1,160]{2,1,0:T(2,128)(2,1)S(1)}, bf16[6,1,160]{2,1,0:T(2,128)(2,1)S(1)}, u32[]{:S(2)}, u32[]{:S(2)}) collective-permute-start(bf16[6,1,160]{2,1,0:T(2,128)(2,1)S(1)} %get-tuple-element.49), channel_id=1, source_target_pairs={{0,1},{1,2},{2,3},{3,4},{4,5},{5,6},{6,7},{8,9},{9,10},{10,11},{11... | collective-permute-start | bytes 5768 | tf_op jit(solution)/shard_map/ppermute | solution.py:23
  43.3 0.6 copy-start.4
  43.4 0.7 copy-start.10
  44.3 0.8 copy-start.14
  45.9 11.4 %collective-permute-start.8 = (bf16[1,32,512]{2,1,0:T(8,128)(2,1)S(1)}, bf16[1,32,512]{2,1,0:T(8,128)(2,1)S(1)}, u32[]{:S(2)}, u32[]{:S(2)}) collective-permute-start(bf16[1,32,512]{2,1,0:T(8,128)(2,1)S(1)} %get-tuple-element.32), channel_id=1, source_target_pairs={{0,8},{8,16},{16,24},{1,9},{9,17},{17,25},{2,10},{10,18},{18,26},{... | collective-permute-start | bytes 98312 | tf_op jit(solution)/shard_map/ppermute | solution.py:23
  49.3 8.0 %collective-permute-start.9 = (bf16[1,32,512]{2,1,0:T(8,128)(2,1)S(1)}, bf16[1,32,512]{2,1,0:T(8,128)(2,1)S(1)}, u32[]{:S(2)}, u32[]{:S(2)}) collective-permute-start(bf16[1,32,512]{2,1,0:T(8,128)(2,1)S(1)} %get-tuple-element.33), channel_id=1, source_target_pairs={{8,0},{16,8},{24,16},{9,1},{17,9},{25,17},{10,2},{18,10},{26,18},{... | collective-permute-start | bytes 98312 | tf_op jit(solution)/shard_map/ppermute | solution.py:25
  57.1 5.9 %copy-start.5 = (bf16[4,32,160]{2,1,0:T(8,128)(2,1)S(1)}, bf16[4,32,160]{2,1,0:T(8,128)(2,1)}, u32[]{:S(2)}) copy-start(bf16[4,32,160]{2,1,0:T(8,128)(2,1)} %copy-done.4) | copy-start | bytes 122884
  57.1 5.9 %copy-start.7 = (bf16[4,32,160]{2,1,0:T(8,128)(2,1)S(1)}, bf16[4,32,160]{2,1,0:T(8,128)(2,1)}, u32[]{:S(2)}) copy-start(bf16[4,32,160]{2,1,0:T(8,128)(2,1)} %copy-done.6) | copy-start | bytes 122884
  57.1 5.9 %copy-start.9 = (bf16[4,32,160]{2,1,0:T(8,128)(2,1)S(1)}, bf16[4,32,160]{2,1,0:T(8,128)(2,1)}, u32[]{:S(2)}) copy-start(bf16[4,32,160]{2,1,0:T(8,128)(2,1)} %copy-done.8) | copy-start | bytes 122884
  57.1 5.9 %copy-start.11 = (bf16[4,32,160]{2,1,0:T(8,128)(2,1)S(1)}, bf16[4,32,160]{2,1,0:T(8,128)(2,1)}, u32[]{:S(2)}) copy-start(bf16[4,32,160]{2,1,0:T(8,128)(2,1)} %copy-done.10) | copy-start | bytes 122884
  57.4 5.9 %collective-permute-start.11 = (bf16[6,1,512]{2,1,0:T(2,128)(2,1)S(1)}, bf16[6,1,512]{2,1,0:T(2,128)(2,1)S(1)}, u32[]{:S(2)}, u32[]{:S(2)}) collective-permute-start(bf16[6,1,512]{2,1,0:T(2,128)(2,1)S(1)} %get-tuple-element.28), channel_id=1, source_target_pairs={{0,1},{1,2},{2,3},{3,4},{4,5},{5,6},{6,7},{8,9},{9,10},{10,11},{11... | collective-permute-start | bytes 18440 | tf_op jit(solution)/shard_map/ppermute | solution.py:23
  61.6 5.1 %collective-permute-start.10 = (bf16[6,1,512]{2,1,0:T(2,128)(2,1)S(1)}, bf16[6,1,512]{2,1,0:T(2,128)(2,1)S(1)}, u32[]{:S(2)}, u32[]{:S(2)}) collective-permute-start(bf16[6,1,512]{2,1,0:T(2,128)(2,1)S(1)} %get-tuple-element.29), channel_id=1, source_target_pairs={{1,0},{2,1},{3,2},{4,3},{5,4},{6,5},{7,6},{9,8},{10,9},{11,10},{12... | collective-permute-start | bytes 18440 | tf_op jit(solution)/shard_map/ppermute | solution.py:25
  66.9 1.4 copy-start.1
  66.9 1.4 copy-start.15
  68.3 1.1 copy-start.13
  69.5 51.0 %collective-permute-start.12 = (bf16[1,32,512]{2,1,0:T(8,128)(2,1)S(1)}, bf16[1,32,512]{2,1,0:T(8,128)(2,1)S(1)}, u32[]{:S(2)}, u32[]{:S(2)}) collective-permute-start(bf16[1,32,512]{2,1,0:T(8,128)(2,1)S(1)} %get-tuple-element.30), channel_id=1, source_target_pairs={{0,8},{8,16},{16,24},{1,9},{9,17},{17,25},{2,10},{10,18},{18,26},{... | collective-permute-start | bytes 98312 | tf_op jit(solution)/shard_map/ppermute | solution.py:23
  74.0 46.5 %collective-permute-start.13 = (bf16[1,32,512]{2,1,0:T(8,128)(2,1)S(1)}, bf16[1,32,512]{2,1,0:T(8,128)(2,1)S(1)}, u32[]{:S(2)}, u32[]{:S(2)}) collective-permute-start(bf16[1,32,512]{2,1,0:T(8,128)(2,1)S(1)} %get-tuple-element.31), channel_id=1, source_target_pairs={{8,0},{16,8},{24,16},{9,1},{17,9},{25,17},{10,2},{18,10},{26,18},{... | collective-permute-start | bytes 98312 | tf_op jit(solution)/shard_map/ppermute | solution.py:25
  120.5 3.2 %collective-permute-start.15 = (bf16[6,1,512]{2,1,0:T(2,128)(2,1)S(1)}, bf16[6,1,512]{2,1,0:T(2,128)(2,1)S(1)}, u32[]{:S(2)}, u32[]{:S(2)}) collective-permute-start(bf16[6,1,512]{2,1,0:T(2,128)(2,1)S(1)} %get-tuple-element.24), channel_id=1, source_target_pairs={{0,1},{1,2},{2,3},{3,4},{4,5},{5,6},{6,7},{8,9},{9,10},{10,11},{11... | collective-permute-start | bytes 18440 | tf_op jit(solution)/shard_map/ppermute | solution.py:23
  121.8 3.9 %collective-permute-start.14 = (bf16[6,1,512]{2,1,0:T(2,128)(2,1)S(1)}, bf16[6,1,512]{2,1,0:T(2,128)(2,1)S(1)}, u32[]{:S(2)}, u32[]{:S(2)}) collective-permute-start(bf16[6,1,512]{2,1,0:T(2,128)(2,1)S(1)} %get-tuple-element.25), channel_id=1, source_target_pairs={{1,0},{2,1},{3,2},{4,3},{5,4},{6,5},{7,6},{9,8},{10,9},{11,10},{12... | collective-permute-start | bytes 18440 | tf_op jit(solution)/shard_map/ppermute | solution.py:25
  125.8 1.4 copy-start.2
  (2 other events, 1.2 us)
Sparse Core Ops, SparseCore 0:
  123.8 140.0 all-reduce.1
where the time goes:
time: 276 us; the launch traced here: 275 us
  waiting for transfers between devices  150 us (54%)
  blocking collectives  42.4 us (15%)
  starting transfers between devices  39.2 us (14%)
  between operations  14.7 us (5%)
  local copies, waits for them, and re-layouts  12.7 us (5%)
  other arithmetic  9.56 us (3%)
  matrix products  5.7 us (2%)
    psum x1, waiting for transfers between devices, shards(): lax.psum((kernel_acc, bias_acc), ('rows', 'cols'))  136 us
    psum x1, blocking collectives, shards(): lax.psum((kernel_acc, bias_acc), ('rows', 'cols'))  42.4 us
    ppermute x8, starting transfers between devices, extended(): lax.ppermute(tail, axis, [(i, (i + 1) % count) for i in range(ends)])  28.8 us
    ppermute x8, waiting for transfers between devices, extended(): lax.ppermute(head, axis, [((i + 1) % count, i) for i in range(ends)])  14 us
    ppermute x8, starting transfers between devices, extended(): lax.ppermute(head, axis, [((i + 1) % count, i) for i in range(ends)])  10.3 us
  transfers between devices with their start and end apart: 17, of which 6 were waited for; matrix products, arithmetic and copies ran while one was open for 5% of the time, Pallas kernels for 0%

commit v1 on v0

--- a/solution.py
+++ b/solution.py
@@ -98,7 +98,7 @@
         grad_hidden = grad_stacked[..., CI:]
         if moment > 0:
             grad_hidden = grad_hidden + cotangent[moment - 1].astype(jnp.float32)
-    kernel_total, bias_total = lax.psum((kernel_acc, bias_acc), ("rows", "cols"))
+    kernel_total, bias_total = lax.psum(lax.psum((kernel_acc, bias_acc), "cols"), "rows")
     total_cells = STEPS * rows_dev * lax.axis_size("rows") * cols_dev * lax.axis_size("cols")
     norm_scale = 1.0 / math.sqrt(total_cells)
     return (hidden, grad_hidden, grad_cell, kernel_total * norm_scale, bias_total * norm_scale)

time: 276 us -> 249 us (0.902)
  blocking collectives: 42.4 us -> 25.3 us
  waiting for transfers between devices: 150 us -> 143 us
    psum x1 -> x2, blocking collectives: 42.4 us -> 25.3 us  [the longest x1 14.6 us: shards(): lax.psum((kernel_acc, bias_acc), 'cols')]
    psum x1 -> x2, waiting for transfers between devices: 136 us -> 128 us  [the longest x1 77.8 us: shards(): lax.psum((kernel_acc, bias_acc), 'cols')]
  transfers between devices with their start and end apart: 17 -> 18, of which waited for: 6 -> 8; matrix products, arithmetic and copies ran while one was open for 5% -> 4% of each run, Pallas kernels for 0% -> 0%
where the time goes in v1:
time: 249 us; the launch traced here: 248 us
  waiting for transfers between devices  143 us (57%)
  starting transfers between devices  36.9 us (15%)
  blocking collectives  25.3 us (10%)
  between operations  14.7 us (6%)
  local copies, waits for them, and re-layouts  12.8 us (5%)
  other arithmetic  9.56 us (4%)
  matrix products  5.7 us (2%)
    psum x1, waiting for transfers between devices, shards(): lax.psum((kernel_acc, bias_acc), 'cols')  77.8 us
    psum x1, waiting for transfers between devices, shards(): lax.psum(lax.psum((kernel_acc, bias_acc), 'cols'), 'rows')  49.9 us
    ppermute x8, starting transfers between devices, extended(): lax.ppermute(tail, axis, [(i, (i + 1) % count) for i in range(ends)])  26.5 us
    psum x1, blocking collectives, shards(): lax.psum((kernel_acc, bias_acc), 'cols')  14.6 us
    ppermute x8, waiting for transfers between devices, extended(): lax.ppermute(head, axis, [((i + 1) % count, i) for i in range(ends)])  13.9 us
    psum x1, blocking collectives, shards(): lax.psum(lax.psum((kernel_acc, bias_acc), 'cols'), 'rows')  10.7 us
    ppermute x8, starting transfers between devices, extended(): lax.ppermute(head, axis, [((i + 1) % count, i) for i in range(ends)])  10.3 us
  transfers between devices with their start and end apart: 18, of which 8 were waited for; matrix products, arithmetic and copies ran while one was open for 4% of the time, Pallas kernels for 0%

profile of v1, /device:TPU:0, one launch (start us, length us, event | category | flops | bytes accessed | tf_op | source)
XLA Modules:
  0.0 247.6 jit_solution(15458851127842841634)
XLA Ops:
  8.8 4.8 %collective-permute-start = (bf16[1,32,160]{2,1,0:T(8,128)(2,1)S(1)}, bf16[1,32,160]{2,1,0:T(8,128)(2,1)S(1)}, u32[]{:S(2)}, u32[]{:S(2)}) collective-permute-start(bf16[1,32,160]{2,1,0:T(8,128)(2,1)S(1)} %get-tuple-element.60), channel_id=1, source_target_pairs={{0,8},{8,16},{16,24},{1,9},{9,17},{17,25},{2,10},{10,18},{18,26},{... | collective-permute-start | bytes 30728 | tf_op jit(solution)/shard_map/ppermute | solution.py:23
  13.7 1.3 collective-permute-start.1
  15.2 4.1 %collective-permute-done.1 = bf16[1,32,160]{2,1,0:T(8,128)(2,1)S(1)} collective-permute-done((bf16[1,32,160]{2,1,0:T(8,128)(2,1)S(1)}, bf16[1,32,160]{2,1,0:T(8,128)(2,1)S(1)}, u32[]{:S(2)}, u32[]{:S(2)}) %collective-permute-start.1) | collective-permute-done | bytes 10272 | tf_op jit(solution)/shard_map/ppermute | solution.py:25
  20.1 1.3 collective-permute-start.3
  21.4 3.2 %collective-permute-start.2 = (bf16[6,1,160]{2,1,0:T(2,128)(2,1)S(1)}, bf16[6,1,160]{2,1,0:T(2,128)(2,1)S(1)}, u32[]{:S(2)}, u32[]{:S(2)}) collective-permute-start(bf16[6,1,160]{2,1,0:T(2,128)(2,1)S(1)} %get-tuple-element.53), channel_id=1, source_target_pairs={{0,1},{1,2},{2,3},{3,4},{4,5},{5,6},{6,7},{8,9},{9,10},{10,11},{11... | collective-permute-start | bytes 5768 | tf_op jit(solution)/shard_map/ppermute | solution.py:23
  27.9 4.3 %collective-permute-start.4 = (bf16[1,32,160]{2,1,0:T(8,128)(2,1)S(1)}, bf16[1,32,160]{2,1,0:T(8,128)(2,1)S(1)}, u32[]{:S(2)}, u32[]{:S(2)}) collective-permute-start(bf16[1,32,160]{2,1,0:T(8,128)(2,1)S(1)} %get-tuple-element.56), channel_id=1, source_target_pairs={{0,8},{8,16},{16,24},{1,9},{9,17},{17,25},{2,10},{10,18},{18,26},{... | collective-permute-start | bytes 30728 | tf_op jit(solution)/shard_map/ppermute | solution.py:23
  32.2 1.3 collective-permute-start.5
  33.6 4.3 %collective-permute-done.5 = bf16[1,32,160]{2,1,0:T(8,128)(2,1)S(1)} collective-permute-done((bf16[1,32,160]{2,1,0:T(8,128)(2,1)S(1)}, bf16[1,32,160]{2,1,0:T(8,128)(2,1)S(1)}, u32[]{:S(2)}, u32[]{:S(2)}) %collective-permute-start.5) | collective-permute-done | bytes 10272 | tf_op jit(solution)/shard_map/ppermute | solution.py:25
  38.0 1.3 collective-permute-start.7
  39.3 3.0 %collective-permute-start.6 = (bf16[6,1,160]{2,1,0:T(2,128)(2,1)S(1)}, bf16[6,1,160]{2,1,0:T(2,128)(2,1)S(1)}, u32[]{:S(2)}, u32[]{:S(2)}) collective-permute-start(bf16[6,1,160]{2,1,0:T(2,128)(2,1)S(1)} %get-tuple-element.49), channel_id=1, source_target_pairs={{0,1},{1,2},{2,3},{3,4},{4,5},{5,6},{6,7},{8,9},{9,10},{10,11},{11... | collective-permute-start | bytes 5768 | tf_op jit(solution)/shard_map/ppermute | solution.py:23
  45.9 3.4 %collective-permute-start.8 = (bf16[1,32,512]{2,1,0:T(8,128)(2,1)S(1)}, bf16[1,32,512]{2,1,0:T(8,128)(2,1)S(1)}, u32[]{:S(2)}, u32[]{:S(2)}) collective-permute-start(bf16[1,32,512]{2,1,0:T(8,128)(2,1)S(1)} %get-tuple-element.32), channel_id=1, source_target_pairs={{0,8},{8,16},{16,24},{1,9},{9,17},{17,25},{2,10},{10,18},{18,26},{... | collective-permute-start | bytes 98312 | tf_op jit(solution)/shard_map/ppermute | solution.py:23
  49.3 1.3 collective-permute-start.9
  50.9 4.2 %collective-permute-done.9 = bf16[1,32,512]{2,1,0:T(8,128)(2,1)S(1)} collective-permute-done((bf16[1,32,512]{2,1,0:T(8,128)(2,1)S(1)}, bf16[1,32,512]{2,1,0:T(8,128)(2,1)S(1)}, u32[]{:S(2)}, u32[]{:S(2)}) %collective-permute-start.9) | collective-permute-done | bytes 32800 | tf_op jit(solution)/shard_map/ppermute | solution.py:25
  55.2 3.1 %collective-permute-start.11 = (bf16[6,1,512]{2,1,0:T(2,128)(2,1)S(1)}, bf16[6,1,512]{2,1,0:T(2,128)(2,1)S(1)}, u32[]{:S(2)}, u32[]{:S(2)}) collective-permute-start(bf16[6,1,512]{2,1,0:T(2,128)(2,1)S(1)} %get-tuple-element.28), channel_id=1, source_target_pairs={{0,1},{1,2},{2,3},{3,4},{4,5},{5,6},{6,7},{8,9},{9,10},{10,11},{11... | collective-permute-start | bytes 18440 | tf_op jit(solution)/shard_map/ppermute | solution.py:23
  58.3 1.3 collective-permute-start.10
  59.6 2.5 copy.14
  62.0 4.0 %reshape.83 = bf16[4608,160,1]{0,1,2:T(8,128)(2,1)} reshape(bf16[9,512,160]{1,0,2:T(8,128)(2,1)} %bitcast.57) | data formatting | bytes 2949120 | tf_op jit(solution)/shard_map/reshape | solution.py:74
  67.1 1.0 copy-done.1
  68.1 1.1 fusion.46
  69.9 2.2 fusion
  72.1 77.8 %all-reduce.3.cloned.1.call-done = f32[1440,512]{1,0:T(8,128)} async-done(((f32[1440,512]{1,0:T(8,128)}), f32[1440,512]{1,0:T(8,128)}) %all-reduce.3.cloned.1.call-update) | async-done | bytes 2949136 | tf_op jit(solution)/shard_map/psum | solution.py:101
  150.0 3.4 %collective-permute-start.12 = (bf16[1,32,512]{2,1,0:T(8,128)(2,1)S(1)}, bf16[1,32,512]{2,1,0:T(8,128)(2,1)S(1)}, u32[]{:S(2)}, u32[]{:S(2)}) collective-permute-start(bf16[1,32,512]{2,1,0:T(8,128)(2,1)S(1)} %get-tuple-element.30), channel_id=1, source_target_pairs={{0,8},{8,16},{16,24},{1,9},{9,17},{17,25},{2,10},{10,18},{18,26},{... | collective-permute-start | bytes 98312 | tf_op jit(solution)/shard_map/ppermute | solution.py:23
  153.4 1.3 collective-permute-start.13
  154.8 14.6 %psum.30 = f32[512]{0:T(512)S(1)} all-reduce(f32[512]{0:T(512)S(1)} %add.72), channel_id=1, replica_groups=mesh['rows'=4,'cols'=8] {'cols'}, use_global_device_ids=true, to_apply=%region_4.0 | all-reduce | flops 512 | bytes 4096 | tf_op jit(solution)/shard_map/psum | solution.py:101
  169.3 10.7 %psum.31 = f32[512]{0:T(512)S(1)} all-reduce(f32[512]{0:T(512)S(1)} %psum.30), channel_id=1, replica_groups=mesh['rows'=4,'cols'=8] {'rows'}, use_global_device_ids=true, to_apply=%region_5.0 | all-reduce | flops 512 | bytes 4096 | tf_op jit(solution)/shard_map/psum | solution.py:101
  180.1 1.3 collective-permute-start.15
  181.4 1.3 collective-permute-start.14
  183.3 1.2 collective-permute-done.14
  184.9 1.1 copy-done.2
  185.9 1.1 fusion.1
  187.0 49.9 %all-reduce.5.cloned.1.call-done = f32[1440,512]{1,0:T(8,128)} async-done(((f32[1440,512]{1,0:T(8,128)}), f32[1440,512]{1,0:T(8,128)}) %all-reduce.5.cloned.1.call-update) | async-done | bytes 2949136 | tf_op jit(solution)/shard_map/psum | solution.py:101
  237.0 3.8 %broadcast_multiply_fusion = f32[1440,512]{1,0:T(8,128)} fusion(f32[1440,512]{1,0:T(8,128)} %all-reduce.5.cloned.1.call-done), kind=kLoop, calls=%fused_computation.4 | loop fusion | flops 737280 | bytes 5898240 | tf_op jit(solution)/shard_map/mul | solution.py:104
  (109 shorter events, 12.4 us)
Async XLA Ops:
  7.2 19.4 %copy-start.3 = (bf16[4,32,128]{2,1,0:T(8,128)(2,1)S(1)}, bf16[4,32,128]{2,1,0:T(8,128)(2,1)}, u32[]{:S(2)}) copy-start(bf16[4,32,128]{2,1,0:T(8,128)(2,1)} %param.7) | copy-start | bytes 98308
  7.2 142.8 %all-reduce.3.cloned.1.call-start = ((), (), s32[]{:S(2)}) async-start(), calls=%async_computation | async-start | bytes 5898240 | tf_op jit(solution)/shard_map/psum | solution.py:101
  8.8 6.3 %collective-permute-start = (bf16[1,32,160]{2,1,0:T(8,128)(2,1)S(1)}, bf16[1,32,160]{2,1,0:T(8,128)(2,1)S(1)}, u32[]{:S(2)}, u32[]{:S(2)}) collective-permute-start(bf16[1,32,160]{2,1,0:T(8,128)(2,1)S(1)} %get-tuple-element.60), channel_id=1, source_target_pairs={{0,8},{8,16},{16,24},{1,9},{9,17},{17,25},{2,10},{10,18},{18,26},{... | collective-permute-start | bytes 30728 | tf_op jit(solution)/shard_map/ppermute | solution.py:23
  13.7 5.6 %collective-permute-start.1 = (bf16[1,32,160]{2,1,0:T(8,128)(2,1)S(1)}, bf16[1,32,160]{2,1,0:T(8,128)(2,1)S(1)}, u32[]{:S(2)}, u32[]{:S(2)}) collective-permute-start(bf16[1,32,160]{2,1,0:T(8,128)(2,1)S(1)} %get-tuple-element.61), channel_id=1, source_target_pairs={{8,0},{16,8},{24,16},{9,1},{17,9},{25,17},{10,2},{18,10},{26,18},{... | collective-permute-start | bytes 30728 | tf_op jit(solution)/shard_map/ppermute | solution.py:25
  20.1 5.4 %collective-permute-start.3 = (bf16[6,1,160]{2,1,0:T(2,128)(2,1)S(1)}, bf16[6,1,160]{2,1,0:T(2,128)(2,1)S(1)}, u32[]{:S(2)}, u32[]{:S(2)}) collective-permute-start(bf16[6,1,160]{2,1,0:T(2,128)(2,1)S(1)} %get-tuple-element.52), channel_id=1, source_target_pairs={{1,0},{2,1},{3,2},{4,3},{5,4},{6,5},{7,6},{9,8},{10,9},{11,10},{12... | collective-permute-start | bytes 5768 | tf_op jit(solution)/shard_map/ppermute | solution.py:25
  21.4 5.4 %copy-start = (bf16[1440,512]{1,0:T(8,128)(2,1)S(1)}, bf16[1440,512]{1,0:T(8,128)(2,1)}, u32[]{:S(2)}) copy-start(bf16[1440,512]{1,0:T(8,128)(2,1)} %param.9) | copy-start | bytes 4423684
  21.4 5.4 %copy-start.16 = (f32[512]{0:T(512)S(1)}, f32[512]{0:T(512)}, u32[]{:S(2)}) copy-start(f32[512]{0:T(512)} %param.10) | copy-start | bytes 6148
  21.4 4.1 %collective-permute-start.2 = (bf16[6,1,160]{2,1,0:T(2,128)(2,1)S(1)}, bf16[6,1,160]{2,1,0:T(2,128)(2,1)S(1)}, u32[]{:S(2)}, u32[]{:S(2)}) collective-permute-start(bf16[6,1,160]{2,1,0:T(2,128)(2,1)S(1)} %get-tuple-element.53), channel_id=1, source_target_pairs={{0,1},{1,2},{2,3},{3,4},{4,5},{5,6},{6,7},{8,9},{9,10},{10,11},{11... | collective-permute-start | bytes 5768 | tf_op jit(solution)/shard_map/ppermute | solution.py:23
  26.9 0.8 copy-start.12
  27.9 5.7 %collective-permute-start.4 = (bf16[1,32,160]{2,1,0:T(8,128)(2,1)S(1)}, bf16[1,32,160]{2,1,0:T(8,128)(2,1)S(1)}, u32[]{:S(2)}, u32[]{:S(2)}) collective-permute-start(bf16[1,32,160]{2,1,0:T(8,128)(2,1)S(1)} %get-tuple-element.56), channel_id=1, source_target_pairs={{0,8},{8,16},{16,24},{1,9},{9,17},{17,25},{2,10},{10,18},{18,26},{... | collective-permute-start | bytes 30728 | tf_op jit(solution)/shard_map/ppermute | solution.py:23
  32.2 5.8 %collective-permute-start.5 = (bf16[1,32,160]{2,1,0:T(8,128)(2,1)S(1)}, bf16[1,32,160]{2,1,0:T(8,128)(2,1)S(1)}, u32[]{:S(2)}, u32[]{:S(2)}) collective-permute-start(bf16[1,32,160]{2,1,0:T(8,128)(2,1)S(1)} %get-tuple-element.57), channel_id=1, source_target_pairs={{8,0},{16,8},{24,16},{9,1},{17,9},{25,17},{10,2},{18,10},{26,18},{... | collective-permute-start | bytes 30728 | tf_op jit(solution)/shard_map/ppermute | solution.py:25
  38.0 4.4 %collective-permute-start.7 = (bf16[6,1,160]{2,1,0:T(2,128)(2,1)S(1)}, bf16[6,1,160]{2,1,0:T(2,128)(2,1)S(1)}, u32[]{:S(2)}, u32[]{:S(2)}) collective-permute-start(bf16[6,1,160]{2,1,0:T(2,128)(2,1)S(1)} %get-tuple-element.48), channel_id=1, source_target_pairs={{1,0},{2,1},{3,2},{4,3},{5,4},{6,5},{7,6},{9,8},{10,9},{11,10},{12... | collective-permute-start | bytes 5768 | tf_op jit(solution)/shard_map/ppermute | solution.py:25
  39.3 3.8 %collective-permute-start.6 = (bf16[6,1,160]{2,1,0:T(2,128)(2,1)S(1)}, bf16[6,1,160]{2,1,0:T(2,128)(2,1)S(1)}, u32[]{:S(2)}, u32[]{:S(2)}) collective-permute-start(bf16[6,1,160]{2,1,0:T(2,128)(2,1)S(1)} %get-tuple-element.49), channel_id=1, source_target_pairs={{0,1},{1,2},{2,3},{3,4},{4,5},{5,6},{6,7},{8,9},{9,10},{10,11},{11... | collective-permute-start | bytes 5768 | tf_op jit(solution)/shard_map/ppermute | solution.py:23
  43.4 0.7 copy-start.10
  44.3 0.8 copy-start.14
  45.9 5.0 %collective-permute-start.8 = (bf16[1,32,512]{2,1,0:T(8,128)(2,1)S(1)}, bf16[1,32,512]{2,1,0:T(8,128)(2,1)S(1)}, u32[]{:S(2)}, u32[]{:S(2)}) collective-permute-start(bf16[1,32,512]{2,1,0:T(8,128)(2,1)S(1)} %get-tuple-element.32), channel_id=1, source_target_pairs={{0,8},{8,16},{16,24},{1,9},{9,17},{17,25},{2,10},{10,18},{18,26},{... | collective-permute-start | bytes 98312 | tf_op jit(solution)/shard_map/ppermute | solution.py:23
  49.3 5.8 %collective-permute-start.9 = (bf16[1,32,512]{2,1,0:T(8,128)(2,1)S(1)}, bf16[1,32,512]{2,1,0:T(8,128)(2,1)S(1)}, u32[]{:S(2)}, u32[]{:S(2)}) collective-permute-start(bf16[1,32,512]{2,1,0:T(8,128)(2,1)S(1)} %get-tuple-element.33), channel_id=1, source_target_pairs={{8,0},{16,8},{24,16},{9,1},{17,9},{25,17},{10,2},{18,10},{26,18},{... | collective-permute-start | bytes 98312 | tf_op jit(solution)/shard_map/ppermute | solution.py:25
  55.2 11.4 %collective-permute-start.11 = (bf16[6,1,512]{2,1,0:T(2,128)(2,1)S(1)}, bf16[6,1,512]{2,1,0:T(2,128)(2,1)S(1)}, u32[]{:S(2)}, u32[]{:S(2)}) collective-permute-start(bf16[6,1,512]{2,1,0:T(2,128)(2,1)S(1)} %get-tuple-element.28), channel_id=1, source_target_pairs={{0,1},{1,2},{2,3},{3,4},{4,5},{5,6},{6,7},{8,9},{9,10},{10,11},{11... | collective-permute-start | bytes 18440 | tf_op jit(solution)/shard_map/ppermute | solution.py:23
  58.3 8.4 %collective-permute-start.10 = (bf16[6,1,512]{2,1,0:T(2,128)(2,1)S(1)}, bf16[6,1,512]{2,1,0:T(2,128)(2,1)S(1)}, u32[]{:S(2)}, u32[]{:S(2)}) collective-permute-start(bf16[6,1,512]{2,1,0:T(2,128)(2,1)S(1)} %get-tuple-element.29), channel_id=1, source_target_pairs={{1,0},{2,1},{3,2},{4,3},{5,4},{6,5},{7,6},{9,8},{10,9},{11,10},{12... | collective-permute-start | bytes 18440 | tf_op jit(solution)/shard_map/ppermute | solution.py:25
  62.0 4.3 %copy-start.5 = (bf16[4,32,160]{2,1,0:T(8,128)(2,1)S(1)}, bf16[4,32,160]{2,1,0:T(8,128)(2,1)}, u32[]{:S(2)}) copy-start(bf16[4,32,160]{2,1,0:T(8,128)(2,1)} %copy-done.4) | copy-start | bytes 122884
  62.0 4.3 %copy-start.7 = (bf16[4,32,160]{2,1,0:T(8,128)(2,1)S(1)}, bf16[4,32,160]{2,1,0:T(8,128)(2,1)}, u32[]{:S(2)}) copy-start(bf16[4,32,160]{2,1,0:T(8,128)(2,1)} %copy-done.6) | copy-start | bytes 122884
  62.0 4.3 %copy-start.9 = (bf16[4,32,160]{2,1,0:T(8,128)(2,1)S(1)}, bf16[4,32,160]{2,1,0:T(8,128)(2,1)}, u32[]{:S(2)}) copy-start(bf16[4,32,160]{2,1,0:T(8,128)(2,1)} %copy-done.8) | copy-start | bytes 122884
  62.0 4.3 %copy-start.11 = (bf16[4,32,160]{2,1,0:T(8,128)(2,1)S(1)}, bf16[4,32,160]{2,1,0:T(8,128)(2,1)}, u32[]{:S(2)}) copy-start(bf16[4,32,160]{2,1,0:T(8,128)(2,1)} %copy-done.10) | copy-start | bytes 122884
  66.7 1.4 copy-start.1
  66.8 1.4 copy-start.15
  68.1 1.1 copy-start.13
  72.1 164.9 %all-reduce.5.cloned.1.call-start = ((), (), s32[]{:S(2)}) async-start(), calls=%async_computation.1 | async-start | bytes 5898240 | tf_op jit(solution)/shard_map/psum | solution.py:101
  150.0 30.1 %collective-permute-start.12 = (bf16[1,32,512]{2,1,0:T(8,128)(2,1)S(1)}, bf16[1,32,512]{2,1,0:T(8,128)(2,1)S(1)}, u32[]{:S(2)}, u32[]{:S(2)}) collective-permute-start(bf16[1,32,512]{2,1,0:T(8,128)(2,1)S(1)} %get-tuple-element.30), channel_id=1, source_target_pairs={{0,8},{8,16},{16,24},{1,9},{9,17},{17,25},{2,10},{10,18},{18,26},{... | collective-permute-start | bytes 98312 | tf_op jit(solution)/shard_map/ppermute | solution.py:23
  153.4 26.7 %collective-permute-start.13 = (bf16[1,32,512]{2,1,0:T(8,128)(2,1)S(1)}, bf16[1,32,512]{2,1,0:T(8,128)(2,1)S(1)}, u32[]{:S(2)}, u32[]{:S(2)}) collective-permute-start(bf16[1,32,512]{2,1,0:T(8,128)(2,1)S(1)} %get-tuple-element.31), channel_id=1, source_target_pairs={{8,0},{16,8},{24,16},{9,1},{17,9},{25,17},{10,2},{18,10},{26,18},{... | collective-permute-start | bytes 98312 | tf_op jit(solution)/shard_map/ppermute | solution.py:25
  180.1 3.2 %collective-permute-start.15 = (bf16[6,1,512]{2,1,0:T(2,128)(2,1)S(1)}, bf16[6,1,512]{2,1,0:T(2,128)(2,1)S(1)}, u32[]{:S(2)}, u32[]{:S(2)}) collective-permute-start(bf16[6,1,512]{2,1,0:T(2,128)(2,1)S(1)} %get-tuple-element.24), channel_id=1, source_target_pairs={{0,1},{1,2},{2,3},{3,4},{4,5},{5,6},{6,7},{8,9},{9,10},{10,11},{11... | collective-permute-start | bytes 18440 | tf_op jit(solution)/shard_map/ppermute | solution.py:23
  181.4 3.1 %collective-permute-start.14 = (bf16[6,1,512]{2,1,0:T(2,128)(2,1)S(1)}, bf16[6,1,512]{2,1,0:T(2,128)(2,1)S(1)}, u32[]{:S(2)}, u32[]{:S(2)}) collective-permute-start(bf16[6,1,512]{2,1,0:T(2,128)(2,1)S(1)} %get-tuple-element.25), channel_id=1, source_target_pairs={{1,0},{2,1},{3,2},{4,3},{5,4},{6,5},{7,6},{9,8},{10,9},{11,10},{12... | collective-permute-start | bytes 18440 | tf_op jit(solution)/shard_map/ppermute | solution.py:25
  184.6 1.4 copy-start.2
  (3 other events, 1.9 us)
Sparse Core Ops, SparseCore 0:
  72.2 77.6 all-reduce.2
  153.4 83.5 all-reduce.4
